TPU v7x, 256 devices: a whole 4x4x8 slice. The times are simulated.
256 devices in a mesh: gx: 8 (over y, core), gy: 32 (over z, x).
Axes of the slice: x: 4, y: 4, z: 8, core: 2. Of those that a mesh axis runs over, the one named last changes fastest.
Arguments:
- source_field: float32 [4096, 64, 256], P('gx', 'gy'), may hold values from -6 to 6
- permeability: float32 [4096, 64, 256], P('gx', 'gy'), may hold values from 0.3 to 3
- layer_ids: int32 [256], replicated, may hold values from 0 to 3, as said below
- inverse_fine: float32 [4, 4096, 512], P(None, 'gx'), as said below
- couple_fine: float32 [2, 4, 8], P(None, None, 'gx'), may hold values from 0.35 to 0.7
- inverse_coarse: float32 [4, 4096, 512], P(None, 'gx'), as said below
- couple_coarse: float32 [2, 4, 8], P(None, None, 'gx'), may hold values from 0.35 to 0.7
- owner_map: int32 [32, 1], replicated, may hold values from 0 to 7
Outputs:
- solution_fine: float32 [4096, 64, 256], P('gx', 'gy')
- residual_fine: float32 [4096, 64, 256], P('gx', 'gy')
- solution_coarse: float32 [4096, 32, 256], P('gx', 'gy')
Inputs may be any that keep to these rules, and one draw needn't show every extreme that they name: owner_map names the aggregate of each level-6 plane; every aggregate below 8 holds at least one plane. `layer_ids`: every rock type names the same number of z cells. `inverse_fine`: each block is a positive-definite dense matrix with a diagonal dominating each line solve's coupling. `inverse_coarse`: each block is a positive-definite dense matrix with a diagonal dominating each line solve's coupling.
All inputs are finite; a program needn't handle non-finite values.
Results may differ from a plain program's by a relative error of at most 0.00012.
Values sent between devices are 32-bit elements; how exact they have to be, the bound alone decides.
No kernel may reach another device: no remote copies, remote signals or barrier semaphores. Data moves between devices by JAX's collectives and lax.ppermute only.
A program may use at most 128 MiB of HBM per device.

v0:
```python
import jax
import jax.numpy as jnp
from jax import lax
from jax.sharding import PartitionSpec as P

NSWEEP = 3
PRECISE = lax.Precision.HIGHEST
WEIGHTS = (0.5, 0.5, 0.15, 0.15, 0.05, 0.05)
STORAGE = 0.1


def with_halo(array, sides, width):
    for axis, dim in sides:
        peers, length = (lax.axis_size(axis), array.shape[dim])
        up = [(i, (i + 1) % peers) for i in range(peers - 1)]
        down = [(j, i) for i, j in up]
        last = lax.slice_in_dim(array, length - width, length, axis=dim)
        leading = lax.slice_in_dim(array, 0, width, axis=dim)
        before = lax.ppermute(last, axis, up)
        after = lax.ppermute(leading, axis, down)
        array = jnp.concatenate([before, array, after], axis=dim)
    return array


def neighbours(padded):
    return [
        padded[:-2, 1:-1, 1:-1],
        padded[2:, 1:-1, 1:-1],
        padded[1:-1, :-2, 1:-1],
        padded[1:-1, 2:, 1:-1],
        padded[1:-1, 1:-1, :-2],
        padded[1:-1, 1:-1, 2:],
    ]


def face_terms(padded):
    centre = padded[1:-1, 1:-1, 1:-1]
    return [
        weight * 2.0 * centre * beside / (centre + beside)
        for weight, beside in zip(WEIGHTS, neighbours(padded))
    ]


def apply_operator(padded, face_list):
    centre = padded[1:-1, 1:-1, 1:-1]
    result_sum = STORAGE * centre
    for face_term, beside in zip(face_list, neighbours(padded)):
        result_sum = result_sum + face_term * (centre - beside)
    return result_sum


def padded_depth(field_now):
    return jnp.pad(field_now, ((0, 0), (0, 0), (1, 1)))


def chain_solve(chain_rows):
    blocks_count = chain_rows.shape[0]
    carry_value = jnp.zeros_like(chain_rows[0, 0])
    carry_gain = jnp.zeros_like(chain_rows[0, 0])
    first_parts, first_links, last_parts, last_links = ([], [], [], [])
    for block_index in range(blocks_count):
        pivot_value = 1.0 - chain_rows[block_index, 2] * carry_gain
        first_part = (
            chain_rows[block_index, 0] - chain_rows[block_index, 2] * carry_value
        ) / pivot_value
        first_link = chain_rows[block_index, 4] / pivot_value
        carry_value = (
            chain_rows[block_index, 1]
            - chain_rows[block_index, 3] * carry_value
            + chain_rows[block_index, 3] * carry_gain * first_part
        )
        carry_gain = (
            chain_rows[block_index, 5] + chain_rows[block_index, 3] * carry_gain * first_link
        )
        first_parts.append(first_part)
        first_links.append(first_link)
        last_parts.append(carry_value)
        last_links.append(carry_gain)
    following = jnp.zeros_like(carry_value)
    last_values = [following] * blocks_count
    next_values = [following] * blocks_count
    for block_index in range(blocks_count - 1, -1, -1):
        next_values[block_index] = following
        last_values[block_index] = last_parts[block_index] - last_links[block_index] * following
        following = first_parts[block_index] - first_links[block_index] * following
    previous = [jnp.zeros_like(following)] + last_values[:-1]
    return jnp.stack(
        [
            jnp.stack([previous[block_index], next_values[block_index]])
            for block_index in range(blocks_count)
        ]
    )


def reduced_solve(chain_local):
    packed = chain_local[None]
    everyone = lax.all_gather(packed, "gx", axis=0, tiled=True)
    solved = chain_solve(everyone)
    return lax.dynamic_index_in_dim(solved, lax.axis_index("gx"), 0, keepdims=False)


def line_apply(grouped, matrices, couples):
    values = jnp.einsum("gic,cgm->igm", matrices, grouped, precision=PRECISE)
    group_count, column_count = (values.shape[1], values.shape[2])
    lower_couple = couples[0]
    upper_couple = couples[1]

    def spread(vector):
        return jnp.broadcast_to(vector[:, None], (group_count, column_count)).reshape(
            group_count * column_count
        )

    chain_local = jnp.stack(
        [
            values[0].reshape(-1),
            values[-1].reshape(-1),
            spread(lower_couple * matrices[:, 0, 0]),
            spread(lower_couple * matrices[:, -1, 0]),
            spread(upper_couple * matrices[:, 0, -1]),
            spread(upper_couple * matrices[:, -1, -1]),
        ]
    )
    solved = reduced_solve(chain_local)
    previous = solved[0].reshape(group_count, column_count)
    following = solved[1].reshape(group_count, column_count)
    first_column = jnp.transpose(matrices[:, :, 0])
    last_column = jnp.transpose(matrices[:, :, -1])
    return (
        values
        - (lower_couple[:, None] * previous)[None] * first_column[:, :, None]
        - (upper_couple[:, None] * following)[None] * last_column[:, :, None]
    )


def local(
    source_field,
    permeability,
    layer_ids,
    inverse_fine,
    couple_fine,
    inverse_coarse,
    couple_coarse,
    owner_map,
):
    block_width, planes, depth_cells = source_field.shape
    layers = inverse_fine.shape[0]
    per_layer = depth_cells // layers
    order = jnp.argsort(layer_ids, stable=True)
    restore = jnp.argsort(order, stable=True)
    halo_permeability = with_halo(permeability, (("gx", 0), ("gy", 1)), 1)
    face_list = face_terms(padded_depth(halo_permeability))

    def residual_of(field_now):
        padded = with_halo(field_now, (("gx", 0), ("gy", 1)), 1)
        return source_field - apply_operator(padded_depth(padded), face_list)

    fine_couples = couple_fine[:, :, 0]
    solution = jnp.zeros_like(source_field)
    update = source_field
    for sweep_index in range(NSWEEP):
        if sweep_index > 0:
            update = residual_of(solution)
        ordered = jnp.take(update, order, axis=2).reshape(block_width, planes, layers, per_layer)
        change = line_apply(
            jnp.transpose(ordered, (0, 2, 1, 3)).reshape(block_width, layers, planes * per_layer),
            inverse_fine,
            fine_couples,
        )
        from_shaped = jnp.transpose(
            change.reshape(block_width, layers, planes, per_layer), (0, 2, 1, 3)
        )
        solution = solution + jnp.take(
            from_shaped.reshape(block_width, planes, depth_cells), restore, axis=2
        )
    residual = residual_of(solution)
    coarse = 0.5 * (residual[:, 0::2, :] + residual[:, 1::2, :])
    coarse_sorted = jnp.take(coarse[:, 0, :], order, axis=1).reshape(block_width, layers, per_layer)
    groups = lax.axis_size("gy")
    position = lax.axis_index("gy")
    aggregates = groups // 4
    owners = owner_map[:, 0]
    own_owner = lax.dynamic_index_in_dim(owners, position, 0, keepdims=False)
    selector = (jnp.arange(aggregates, dtype=jnp.int32) == own_owner).astype(jnp.float32)
    slot_terms = selector[None, None, :, None] * coarse_sorted[:, :, None, :]
    flat_terms = slot_terms.reshape(block_width, layers * aggregates * per_layer)
    own_columns = lax.psum_scatter(flat_terms, "gy", scatter_dimension=1, tiled=True)
    own_layer = position // (groups // layers)
    matrix = lax.dynamic_index_in_dim(inverse_coarse, own_layer, 0, keepdims=True)
    couples = lax.dynamic_index_in_dim(couple_coarse[:, :, 0], own_layer, 1, keepdims=True)
    smoothed = line_apply(own_columns[:, None, :], matrix, couples)[:, 0, :]
    every_column = lax.all_gather(smoothed, "gy", axis=1, tiled=True)
    shaped = every_column.reshape(block_width, layers, aggregates, per_layer)
    picked = lax.dynamic_index_in_dim(shaped, own_owner, 2, keepdims=False)
    result = jnp.take(picked.reshape(block_width, depth_cells), restore, axis=1)
    return (solution, residual, result[:, None, :])


def solution(mesh):
    in_specs = (
        P("gx", "gy", None),
        P("gx", "gy", None),
        P(),
        P(None, "gx", None),
        P(None, None, "gx"),
        P(None, "gx", None),
        P(None, None, "gx"),
        P(),
    )
    out_specs = (P("gx", "gy", None), P("gx", "gy", None), P("gx", "gy", None))
    return jax.shard_map(local, mesh=mesh, in_specs=in_specs, out_specs=out_specs, check_vma=False)
```

profile of v0, /device:TPU:8, one launch (start us, length us, event | category | flops | bytes accessed | tf_op | source)
XLA Modules:
  0.0 583.6 jit_solution(3211472923270498532)
XLA Ops:
  7.2 3.8 sort.31
  12.0 2.5 slice_reduce_fusion.1
  14.5 3.2 sort.32
  17.7 2.5 copy.159
  24.2 4.5 convolution_bitcast_fusion.2
  29.3 13.0 %all-gather.5 = f32[8,6,512]{2,1,0:T(8,128)S(1)} all-gather(f32[1,6,512]{2,1,0:T(8,128)S(1)} %bitcast.1530), channel_id=2, replica_groups=mesh['gx'=8,'gy'=32] {'gx'}, dimensions={0}, use_global_device_ids=true | all-gather | bytes 110592 | tf_op jit(solution)/shard_map/all_gather | solution.py:97
  46.6 2.2 collective-permute-start.1
  48.9 3.5 collective-permute-start.3
  52.4 1.9 collective-permute-start
  54.4 3.9 collective-permute-start.2
  59.1 3.3 collective-permute-start.5
  64.9 4.6 collective-permute-start.4
  71.4 3.3 collective-permute-done.5
  74.8 4.9 collective-permute-done.7
  79.7 4.0 collective-permute-done.4
  83.8 4.6 collective-permute-done.6
  88.5 2.1 select_maximum_fusion.8
  90.6 2.1 select_maximum_fusion.12
  94.4 3.6 fusion.37
  99.3 3.0 gather_fusion.2
  104.5 4.5 convolution_bitcast_fusion.1
  109.4 22.6 %all-gather.6 = f32[8,6,512]{2,1,0:T(8,128)S(1)} all-gather(f32[1,6,512]{2,1,0:T(8,128)S(1)} %bitcast.1531), channel_id=3, replica_groups=mesh['gx'=8,'gy'=32] {'gx'}, dimensions={0}, use_global_device_ids=true | all-gather | bytes 110592 | tf_op jit(solution)/shard_map/all_gather | solution.py:97
  133.8 2.7 gather_fusion.3
  136.4 2.3 copy.197
  140.4 2.2 collective-permute-start.8
  142.6 3.3 collective-permute-start.9
  148.0 3.4 collective-permute-start.10
  153.2 10.3 %collective-permute-done.10 = f32[514,1,256]{2,1,0:T(1,128)S(1)} collective-permute-done((f32[514,1,256]{2,1,0:T(1,128)S(1)}, f32[514,1,256]{2,1,0:T(1,128)S(1)}, u32[]{:S(2)}, u32[]{:S(2)}) %collective-permute-start.10) | collective-permute-done | bytes 526368 | tf_op jit(solution)/shard_map/ppermute | solution.py:19
  163.6 4.9 collective-permute-done.11
  168.6 2.1 select_maximum_fusion.4
  170.7 4.5 fusion.20
  176.7 2.7 gather_fusion.4
  179.4 2.2 broadcast_select_fusion
  181.9 4.5 convolution_bitcast_fusion
  186.8 11.7 %all-gather.7 = f32[8,6,512]{2,1,0:T(8,128)S(1)} all-gather(f32[1,6,512]{2,1,0:T(8,128)S(1)} %bitcast.1529), channel_id=4, replica_groups=mesh['gx'=8,'gy'=32] {'gx'}, dimensions={0}, use_global_device_ids=true | all-gather | bytes 110592 | tf_op jit(solution)/shard_map/all_gather | solution.py:97
  201.2 3.0 gather_fusion.5
  207.0 2.2 collective-permute-start.12
  209.3 3.3 collective-permute-start.13
  214.6 5.0 collective-permute-start.14
  223.7 7.9 %collective-permute-done.14 = f32[514,1,256]{2,1,0:T(1,128)S(1)} collective-permute-done((f32[514,1,256]{2,1,0:T(1,128)S(1)}, f32[514,1,256]{2,1,0:T(1,128)S(1)}, u32[]{:S(2)}, u32[]{:S(2)}) %collective-permute-start.14) | collective-permute-done | bytes 526368 | tf_op jit(solution)/shard_map/ppermute | solution.py:19
  231.7 6.3 %collective-permute-done.15 = f32[514,1,256]{2,1,0:T(1,128)} collective-permute-done((f32[514,1,256]{2,1,0:T(1,128)}, f32[514,1,256]{2,1,0:T(1,128)}, u32[]{:S(2)}, u32[]{:S(2)}) %collective-permute-start.15) | collective-permute-done | bytes 526368 | tf_op jit(solution)/shard_map/ppermute | solution.py:20
  239.0 2.1 select_maximum_fusion
  241.2 3.6 fusion.3
  246.2 2.3 bitcast_multiply_fusion
  258.6 216.9 %reduce-scatter.2.cloned.1.call-done = f32[512,64]{0,1:T(8,128)} async-done(((f32[512,2048]{0,1:T(8,128)}), f32[512,64]{0,1:T(8,128)}) %reduce-scatter.2.cloned.1.call-update) | async-done | bytes 131088 | tf_op jit(solution)/shard_map/reduce_scatter | solution.py:186
  475.5 2.0 convolution_bitcast_fusion.3
  477.8 13.1 %all-gather.8 = f32[8,6,64]{2,1,0:T(8,128)S(1)} all-gather(f32[1,6,64]{2,1,0:T(8,128)S(1)} %bitcast.1545), channel_id=5, replica_groups=mesh['gx'=8,'gy'=32] {'gx'}, dimensions={0}, use_global_device_ids=true | all-gather | bytes 13824 | tf_op jit(solution)/shard_map/all_gather | solution.py:97
  498.7 74.4 %all-gather.11.cloned.1.call-done = f32[512,1,2048]{0,2,1:T(8,128)} async-done(((f32[512,1,64]{0,2,1:T(8,128)}), f32[512,1,2048]{0,2,1:T(8,128)}) %all-gather.11.cloned.1.call-update) | async-done | bytes 4194320 | tf_op jit(solution)/shard_map/all_gather | solution.py:191
  (239 shorter events, 58.3 us)
Async XLA Ops:
  7.2 215.1 %copy-start = (s32[32,1]{0,1:T(1,128)S(1)}, s32[32,1]{0,1:T(1,128)}, u32[]{:S(2)}) copy-start(s32[32,1]{0,1:T(1,128)} %param.19) | copy-start | bytes 388
  7.2 468.3 %reduce-scatter.2.cloned.1.call-start = ((), (), s32[]{:S(2)}) async-start(), calls=%async_computation.1 | async-start | bytes 4325376 | tf_op jit(solution)/shard_map/reduce_scatter | solution.py:186
  22.0 2.2 copy-start.1
  24.1 4.8 copy-start.19
  44.1 8.3 %copy-start.7 = (f32[512,2,256]{2,1,0:T(2,128)S(1)}, f32[512,2,256]{2,1,0:T(2,128)}, u32[]{:S(2)}) copy-start(f32[512,2,256]{2,1,0:T(2,128)} %param.13) | copy-start | bytes 3145732
  46.5 7.8 %copy-start.18 = (f32[256,512,2]{0,1,2:T(8,128)}, f32[256,512,2]{0,1,2:T(8,128)S(1)}, u32[]{:S(2)}) copy-start(f32[256,512,2]{0,1,2:T(8,128)S(1)} %copy.164) | copy-start | bytes 3145732
  46.6 11.7 %collective-permute-start.1 = (f32[1,2,256]{2,0,1:T(1,128)S(1)}, f32[1,2,256]{2,0,1:T(1,128)S(1)}, u32[]{:S(2)}, u32[]{:S(2)}) collective-permute-start(f32[1,2,256]{2,0,1:T(1,128)S(1)} %get-tuple-element.218), channel_id=1, source_target_pairs={{0,32},{32,64},{64,96},{96,128},{128,160},{160,192},{192,224},{1,3... | collective-permute-start | bytes 6152 | tf_op jit(solution)/shard_map/ppermute | solution.py:19
  48.9 9.5 %collective-permute-start.3 = (f32[1,2,256]{2,0,1:T(1,128)S(1)}, f32[1,2,256]{2,0,1:T(1,128)S(1)}, u32[]{:S(2)}, u32[]{:S(2)}) collective-permute-start(f32[1,2,256]{2,0,1:T(1,128)S(1)} %get-tuple-element.219), channel_id=1, source_target_pairs={{32,0},{64,32},{96,64},{128,96},{160,128},{192,160},{224,192},{33,... | collective-permute-start | bytes 6152 | tf_op jit(solution)/shard_map/ppermute | solution.py:20
  52.4 11.8 %collective-permute-start = (f32[1,2,256]{2,0,1:T(1,128)S(1)}, f32[1,2,256]{2,0,1:T(1,128)S(1)}, u32[]{:S(2)}, u32[]{:S(2)}) collective-permute-start(f32[1,2,256]{2,0,1:T(1,128)S(1)} %copy.165), channel_id=1, source_target_pairs={{0,32},{32,64},{64,96},{96,128},{128,160},{160,192},{192,224},{1,3... | collective-permute-start | bytes 6152 | tf_op jit(solution)/shard_map/ppermute | solution.py:19
  54.4 9.8 %collective-permute-start.2 = (f32[1,2,256]{2,0,1:T(1,128)S(1)}, f32[1,2,256]{2,0,1:T(1,128)S(1)}, u32[]{:S(2)}, u32[]{:S(2)}) collective-permute-start(f32[1,2,256]{2,0,1:T(1,128)S(1)} %copy.169), channel_id=1, source_target_pairs={{32,0},{64,32},{96,64},{128,96},{160,128},{192,160},{224,192},{33,... | collective-permute-start | bytes 6152 | tf_op jit(solution)/shard_map/ppermute | solution.py:20
  59.1 15.6 %collective-permute-start.5 = (f32[514,1,256]{2,1,0:T(1,128)S(1)}, f32[514,1,256]{2,1,0:T(1,128)S(1)}, u32[]{:S(2)}, u32[]{:S(2)}) collective-permute-start(f32[514,1,256]{2,1,0:T(1,128)S(1)} %copy.178), channel_id=1, source_target_pairs={{0,1},{1,2},{2,3},{3,4},{4,5},{5,6},{6,7},{7,8},{8,9},{9,10},{10,1... | collective-permute-start | bytes 1579016 | tf_op jit(solution)/shard_map/ppermute | solution.py:19
  62.9 16.8 %collective-permute-start.7 = (f32[514,1,256]{2,1,0:T(1,128)S(1)}, f32[514,1,256]{2,1,0:T(1,128)S(1)}, u32[]{:S(2)}, u32[]{:S(2)}) collective-permute-start(f32[514,1,256]{2,1,0:T(1,128)S(1)} %copy.183), channel_id=1, source_target_pairs={{1,0},{2,1},{3,2},{4,3},{5,4},{6,5},{7,6},{8,7},{9,8},{10,9},{11,1... | collective-permute-start | bytes 1579016 | tf_op jit(solution)/shard_map/ppermute | solution.py:20
  64.9 18.8 %collective-permute-start.4 = (f32[514,1,256]{2,1,0:T(1,128)S(1)}, f32[514,1,256]{2,1,0:T(1,128)S(1)}, u32[]{:S(2)}, u32[]{:S(2)}) collective-permute-start(f32[514,1,256]{2,1,0:T(1,128)S(1)} %copy.175), channel_id=1, source_target_pairs={{0,1},{1,2},{2,3},{3,4},{4,5},{5,6},{6,7},{7,8},{8,9},{9,10},{10,1... | collective-permute-start | bytes 1579016 | tf_op jit(solution)/shard_map/ppermute | solution.py:19
  70.1 18.4 %collective-permute-start.6 = (f32[514,1,256]{2,1,0:T(1,128)S(1)}, f32[514,1,256]{2,1,0:T(1,128)S(1)}, u32[]{:S(2)}, u32[]{:S(2)}) collective-permute-start(f32[514,1,256]{2,1,0:T(1,128)S(1)} %copy.180), channel_id=1, source_target_pairs={{1,0},{2,1},{3,2},{4,3},{5,4},{6,5},{7,6},{8,7},{9,8},{10,9},{11,1... | collective-permute-start | bytes 1579016 | tf_op jit(solution)/shard_map/ppermute | solution.py:20
  83.8 9.0 %copy-start.12 = (f32[514,1,256]{2,0,1:T(8,128)}, f32[514,1,256]{2,0,1:T(8,128)S(1)}, u32[]{:S(2)}) copy-start(f32[514,1,256]{2,0,1:T(8,128)S(1)} %copy.176) | copy-start | bytes 1579012
  88.5 4.3 copy-start.15
  90.6 3.8 copy-start.9
  92.8 1.7 copy-start.4
  102.3 2.2 copy-start.2
  140.4 5.6 collective-permute-start.8
  142.6 4.6 collective-permute-start.9
  148.0 15.6 %collective-permute-start.10 = (f32[514,1,256]{2,1,0:T(1,128)S(1)}, f32[514,1,256]{2,1,0:T(1,128)S(1)}, u32[]{:S(2)}, u32[]{:S(2)}) collective-permute-start(f32[514,1,256]{2,1,0:T(1,128)S(1)} %copy.198), channel_id=1, source_target_pairs={{0,1},{1,2},{2,3},{3,4},{4,5},{5,6},{6,7},{7,8},{8,9},{9,10},{10,1... | collective-permute-start | bytes 1579016 | tf_op jit(solution)/shard_map/ppermute | solution.py:19
  151.9 16.6 %collective-permute-start.11 = (f32[514,1,256]{2,1,0:T(1,128)S(1)}, f32[514,1,256]{2,1,0:T(1,128)S(1)}, u32[]{:S(2)}, u32[]{:S(2)}) collective-permute-start(f32[514,1,256]{2,1,0:T(1,128)S(1)} %copy.200), channel_id=1, source_target_pairs={{1,0},{2,1},{3,2},{4,3},{5,4},{6,5},{7,6},{8,7},{9,8},{10,9},{11,1... | collective-permute-start | bytes 1579016 | tf_op jit(solution)/shard_map/ppermute | solution.py:20
  163.6 7.1 %copy-start.5 = (f32[514,4,258]{2,0,1:T(8,128)S(1)}, f32[514,4,258]{2,0,1:T(8,128)}, u32[]{:S(2)}) copy-start(f32[514,4,258]{2,0,1:T(8,128)} %copy-done.4) | copy-start | bytes 6365380
  163.6 7.1 %copy-start.10 = (f32[512,2,256]{2,1,0:T(2,128)S(1)}, f32[512,2,256]{2,1,0:T(2,128)}, u32[]{:S(2)}) copy-start(f32[512,2,256]{2,1,0:T(2,128)} %param.12) | copy-start | bytes 3145732
  163.6 7.1 %copy-start.13 = (f32[514,1,256]{2,0,1:T(8,128)S(1)}, f32[514,1,256]{2,0,1:T(8,128)}, u32[]{:S(2)}) copy-start(f32[514,1,256]{2,0,1:T(8,128)} %copy-done.12) | copy-start | bytes 1579012
  163.6 7.1 %copy-start.16 = (f32[514,1,256]{2,0,1:T(8,128)S(1)}, f32[514,1,256]{2,0,1:T(8,128)}, u32[]{:S(2)}) copy-start(f32[514,1,256]{2,0,1:T(8,128)} %copy-done.15) | copy-start | bytes 1579012
  179.4 2.5 copy-start.3
  207.0 5.6 collective-permute-start.12
  209.3 4.6 collective-permute-start.13
  214.6 17.0 %collective-permute-start.14 = (f32[514,1,256]{2,1,0:T(1,128)S(1)}, f32[514,1,256]{2,1,0:T(1,128)S(1)}, u32[]{:S(2)}, u32[]{:S(2)}) collective-permute-start(f32[514,1,256]{2,1,0:T(1,128)S(1)} %copy.210), channel_id=1, source_target_pairs={{0,1},{1,2},{2,3},{3,4},{4,5},{5,6},{6,7},{7,8},{8,9},{9,10},{10,1... | collective-permute-start | bytes 1579016 | tf_op jit(solution)/shard_map/ppermute | solution.py:19
  221.0 17.0 %collective-permute-start.15 = (f32[514,1,256]{2,1,0:T(1,128)}, f32[514,1,256]{2,1,0:T(1,128)}, u32[]{:S(2)}, u32[]{:S(2)}) collective-permute-start(f32[514,1,256]{2,1,0:T(1,128)} %copy.212), channel_id=1, source_target_pairs={{1,0},{2,1},{3,2},{4,3},{5,4},{6,5},{7,6},{8,7},{9,8},{10,9},{11,1... | collective-permute-start | bytes 1579016 | tf_op jit(solution)/shard_map/ppermute | solution.py:20
  231.6 9.5 %copy-start.6 = (f32[514,4,258]{2,0,1:T(8,128)S(1)}, f32[514,4,258]{2,0,1:T(8,128)}, u32[]{:S(2)}) copy-start(f32[514,4,258]{2,0,1:T(8,128)} %copy-done.4) | copy-start | bytes 6365380
  231.7 9.5 %copy-start.8 = (f32[512,2,256]{2,1,0:T(2,128)S(1)}, f32[512,2,256]{2,1,0:T(2,128)}, u32[]{:S(2)}) copy-start(f32[512,2,256]{2,1,0:T(2,128)} %param.13) | copy-start | bytes 3145732
  231.7 9.5 %copy-start.11 = (f32[512,2,256]{2,1,0:T(2,128)S(1)}, f32[512,2,256]{2,1,0:T(2,128)}, u32[]{:S(2)}) copy-start(f32[512,2,256]{2,1,0:T(2,128)} %param.12) | copy-start | bytes 3145732
  231.7 9.5 %copy-start.14 = (f32[514,1,256]{2,0,1:T(8,128)S(1)}, f32[514,1,256]{2,0,1:T(8,128)}, u32[]{:S(2)}) copy-start(f32[514,1,256]{2,0,1:T(8,128)} %copy-done.12) | copy-start | bytes 1579012
  231.7 9.5 %copy-start.17 = (f32[514,1,256]{2,0,1:T(8,128)S(1)}, f32[514,1,256]{2,0,1:T(8,128)}, u32[]{:S(2)}) copy-start(f32[514,1,256]{2,0,1:T(8,128)} %copy-done.15) | copy-start | bytes 1579012
  248.6 0.7 copy-start.20
  248.6 324.5 %all-gather.11.cloned.1.call-start = ((), (), s32[]{:S(2)}) async-start(), calls=%async_computation.2 | async-start | bytes 4325376 | tf_op jit(solution)/shard_map/all_gather | solution.py:191
Sparse Core Ops, SparseCore 0:
  248.7 226.7 reduce-scatter.1
  493.3 79.6 all-gather.10
where the time goes:
time: 593 us; the launch traced here: 584 us
  waiting for transfers between devices  340 us (57%)
  blocking collectives  60.3 us (10%)
  local copies, waits for them, and re-layouts  57.9 us (10%)
  starting transfers between devices  44.2 us (7%)
  other arithmetic  42.8 us (7%)
  between operations  22.7 us (4%)
  matrix products  15.5 us (3%)
    reduce_scatter x1, waiting for transfers between devices, local(): lax.psum_scatter(flat_terms, 'gy', scatter_dimension=1, tiled=True)  217 us
    all_gather x1, waiting for transfers between devices, local(): every_column = lax.all_gather(smoothed, 'gy', axis=1, tiled=True)  74.4 us
    all_gather x4, blocking collectives, reduced_solve(): everyone = lax.all_gather(packed, 'gx', axis=0, tiled=True)  60.3 us
    ppermute x8, waiting for transfers between devices, with_halo(): before = lax.ppermute(last, axis, up)  25.6 us
    ppermute x8, starting transfers between devices, with_halo(): before = lax.ppermute(last, axis, up)  24.9 us
    ppermute x8, waiting for transfers between devices, with_halo(): after = lax.ppermute(leading, axis, down)  23.3 us
    ppermute x8, starting transfers between devices, with_halo(): after = lax.ppermute(leading, axis, down)  19.2 us
    dot_general x4, matrix products, line_apply(): values = jnp.einsum('gic,cgm->igm', matrices, grouped, precision=PRECISE)  15.5 us
  transfers between devices with their start and end apart: 18, of which 12 were waited for; matrix products, arithmetic and copies ran while one was open for 2% of the time, Pallas kernels for 0%

commit v1 on v0

--- a/solution.py
+++ b/solution.py
@@ -7,6 +7,12 @@
 PRECISE = lax.Precision.HIGHEST
 WEIGHTS = (0.5, 0.5, 0.15, 0.15, 0.05, 0.05)
 STORAGE = 0.1
+
+
+def pack_stops_all(array_in, dim_i):
+    field_out = list(array_in.shape[1:])
+    field_out[dim_i] *= array_in.shape[0]
+    return jnp.moveaxis(array_in, 0, dim_i).reshape(field_out)
 
 
 def with_halo(array, sides, width):
@@ -94,7 +100,23 @@
 
 def reduced_solve(chain_local):
     packed = chain_local[None]
-    everyone = lax.all_gather(packed, "gx", axis=0, tiled=True)
+    n_shards = jax.lax.axis_size("gx")
+    in_order = [(ix, (ix + 1) % n_shards) for ix in range(n_shards)]
+    blocks_here = [(pp, p) for p, pp in in_order]
+    parts_out, response = ([], [])
+    for c in range(n_shards - 1):
+        if c % 2 == 0:
+            parts_out.append(
+                jax.lax.ppermute(parts_out[-1] if parts_out else packed, "gx", in_order)
+            )
+        else:
+            response.append(
+                jax.lax.ppermute(response[-1] if response else packed, "gx", blocks_here)
+            )
+    t1 = jnp.stack([*parts_out[::-1], packed, *response], axis=0)
+    wide_out = jax.lax.axis_index("gx") - len(parts_out)
+    t1 = t1[(jnp.arange(n_shards) - wide_out) % n_shards]
+    everyone = pack_stops_all(t1, 0)
     solved = chain_solve(everyone)
     return lax.dynamic_index_in_dim(solved, lax.axis_index("gx"), 0, keepdims=False)
 

time: 593 us -> 602 us (1.015)
  blocking collectives: 60.3 us -> 0 us
  waiting for transfers between devices: 340 us -> 372 us
  starting transfers between devices: 44.2 us -> 68.1 us
  local copies, waits for them, and re-layouts: 57.9 us -> 70 us
    all_gather x4 -> x0, blocking collectives: 60.3 us -> none  [reduced_solve(): everyone = lax.all_gather(packed, 'gx', axis=0, tiled=True)]
    ppermute x0 -> x28, waiting for transfers between devices: none -> 26.1 us  [the longest x16 24.1 us: reduced_solve(): jax.lax.ppermute(parts_out[-1] if parts_out else packed, 'gx', in_order)]
    ppermute x0 -> x28, starting transfers between devices: none -> 21.2 us  [the longest x12 20.9 us: reduced_solve(): jax.lax.ppermute(response[-1] if response else packed, 'gx', blocks_here)]
    reduce_scatter x1, waiting for transfers between devices: 217 us -> 224 us  [local(): lax.psum_scatter(flat_terms, 'gy', scatter_dimension=1, tiled=True)]
    unnamed x53 -> x93, local copies, waits for them, and re-layouts: 12.5 us -> 15.7 us
  transfers between devices with their start and end apart: 18 -> 46, of which waited for: 12 -> 27; matrix products, arithmetic and copies ran while one was open for 2% -> 6% of each run, Pallas kernels for 0% -> 0%
where the time goes in v1:
time: 602 us; the launch traced here: 594 us
  waiting for transfers between devices  372 us (62%)
  local copies, waits for them, and re-layouts  70 us (12%)
  starting transfers between devices  68.1 us (11%)
  other arithmetic  45.9 us (8%)
  between operations  22.8 us (4%)
  matrix products  15.5 us (3%)
    reduce_scatter x1, waiting for transfers between devices, local(): lax.psum_scatter(flat_terms, 'gy', scatter_dimension=1, tiled=True)  224 us
    all_gather x1, waiting for transfers between devices, local(): every_column = lax.all_gather(smoothed, 'gy', axis=1, tiled=True)  77.1 us
    ppermute x8, starting transfers between devices, with_halo(): before = lax.ppermute(last, axis, up)  27.7 us
    ppermute x8, waiting for transfers between devices, with_halo(): before = lax.ppermute(last, axis, up)  24.5 us
    ppermute x16, waiting for transfers between devices, reduced_solve(): jax.lax.ppermute(parts_out[-1] if parts_out else packed, 'gx', in_order)  24.1 us
    ppermute x12, starting transfers between devices, reduced_solve(): jax.lax.ppermute(response[-1] if response else packed, 'gx', blocks_here)  20.9 us
    ppermute x8, waiting for transfers between devices, with_halo(): after = lax.ppermute(leading, axis, down)  19.6 us
    ppermute x8, starting transfers between devices, with_halo(): after = lax.ppermute(leading, axis, down)  19.2 us
  transfers between devices with their start and end apart: 46, of which 27 were waited for; matrix products, arithmetic and copies ran while one was open for 6% of the time, Pallas kernels for 0%

profile of v1, /device:TPU:8, one launch (start us, length us, event | category | flops | bytes accessed | tf_op | source)
XLA Modules:
  0.0 593.9 jit_solution(16916186709966512093)
XLA Ops:
  7.2 3.8 sort.31
  12.1 2.5 copy.159
  18.5 4.5 convolution_bitcast_fusion.2
  27.4 3.6 collective-permute-start.9
  31.6 2.5 slice_reduce_fusion.1
  34.0 3.2 sort.32
  37.9 3.1 collective-permute-done.1
  45.5 4.2 collective-permute-start.11
  59.1 2.7 gather_fusion.5
  63.3 3.6 collective-permute-start.10
  66.9 2.3 collective-permute-start.8
  69.2 2.6 collective-permute-done.8
  72.6 4.7 collective-permute-start.12
  81.5 2.1 select_maximum_fusion.12
  83.7 4.4 collective-permute-done.12
  88.1 4.6 collective-permute-done.14
  92.8 2.1 select_maximum_fusion.8
  94.9 3.6 fusion.37
  99.9 3.0 gather_fusion.6
  105.1 4.5 convolution_bitcast_fusion.1
  110.0 3.2 collective-permute-done.15
  126.5 2.7 gather_fusion.7
  129.2 2.3 copy.197
  133.1 3.0 collective-permute-start.22
  136.1 2.6 collective-permute-start.23
  140.7 2.6 collective-permute-start.24
  145.2 10.3 %collective-permute-done.24 = f32[514,1,256]{2,1,0:T(1,128)S(1)} collective-permute-done((f32[514,1,256]{2,1,0:T(1,128)S(1)}, f32[514,1,256]{2,1,0:T(1,128)S(1)}, u32[]{:S(2)}, u32[]{:S(2)}) %collective-permute-start.24) | collective-permute-done | bytes 526368 | tf_op jit(solution)/shard_map/ppermute | solution.py:25
  155.6 6.3 %collective-permute-done.25 = f32[514,1,256]{2,1,0:T(1,128)S(1)} collective-permute-done((f32[514,1,256]{2,1,0:T(1,128)S(1)}, f32[514,1,256]{2,1,0:T(1,128)S(1)}, u32[]{:S(2)}, u32[]{:S(2)}) %collective-permute-start.25) | collective-permute-done | bytes 526368 | tf_op jit(solution)/shard_map/ppermute | solution.py:26
  161.9 2.5 select_maximum_fusion.4
  164.4 4.5 fusion.20
  168.9 2.2 copy.205
  171.2 3.0 gather_fusion.8
  176.4 4.5 convolution_bitcast_fusion
  181.3 3.0 collective-permute-done.26
  196.9 2.7 gather_fusion.9
  199.6 2.3 copy.209
  203.3 2.8 collective-permute-start.33
  206.1 4.1 collective-permute-start.34
  212.0 6.2 %collective-permute-start.35 = (f32[514,1,256]{2,1,0:T(1,128)S(1)}, f32[514,1,256]{2,1,0:T(1,128)S(1)}, u32[]{:S(2)}, u32[]{:S(2)}) collective-permute-start(f32[514,1,256]{2,1,0:T(1,128)S(1)} %copy.210), channel_id=1, source_target_pairs={{0,1},{1,2},{2,3},{3,4},{4,5},{5,6},{6,7},{7,8},{8,9},{9,10},{10,1... | collective-permute-start | bytes 1579016 | tf_op jit(solution)/shard_map/ppermute | solution.py:25
  222.2 7.2 %collective-permute-done.35 = f32[514,1,256]{2,1,0:T(1,128)S(1)} collective-permute-done((f32[514,1,256]{2,1,0:T(1,128)S(1)}, f32[514,1,256]{2,1,0:T(1,128)S(1)}, u32[]{:S(2)}, u32[]{:S(2)}) %collective-permute-start.35) | collective-permute-done | bytes 526368 | tf_op jit(solution)/shard_map/ppermute | solution.py:25
  229.5 6.3 %collective-permute-done.36 = f32[514,1,256]{2,1,0:T(1,128)} collective-permute-done((f32[514,1,256]{2,1,0:T(1,128)}, f32[514,1,256]{2,1,0:T(1,128)}, u32[]{:S(2)}, u32[]{:S(2)}) %collective-permute-start.36) | collective-permute-done | bytes 526368 | tf_op jit(solution)/shard_map/ppermute | solution.py:26
  236.9 2.1 select_maximum_fusion
  239.1 3.6 fusion.3
  244.1 2.3 bitcast_multiply_fusion
  254.6 224.2 %reduce-scatter.2.cloned.1.call-done = f32[512,64]{0,1:T(8,128)} async-done(((f32[512,2048]{0,1:T(8,128)}), f32[512,64]{0,1:T(8,128)}) %reduce-scatter.2.cloned.1.call-update) | async-done | bytes 131088 | tf_op jit(solution)/shard_map/reduce_scatter | solution.py:208
  478.8 2.0 convolution_bitcast_fusion.3
  481.1 3.0 collective-permute-done.37
  506.5 77.1 %all-gather.3.cloned.1.call-done = f32[512,1,2048]{0,2,1:T(8,128)} async-done(((f32[512,1,64]{0,2,1:T(8,128)}), f32[512,1,2048]{0,2,1:T(8,128)}) %all-gather.3.cloned.1.call-update) | async-done | bytes 4194320 | tf_op jit(solution)/shard_map/all_gather | solution.py:213
  (341 shorter events, 105.0 us)
Async XLA Ops:
  7.2 213.6 %copy-start = (s32[32,1]{0,1:T(1,128)S(1)}, s32[32,1]{0,1:T(1,128)}, u32[]{:S(2)}) copy-start(s32[32,1]{0,1:T(1,128)} %param.19) | copy-start | bytes 388
  7.2 471.7 %reduce-scatter.2.cloned.1.call-start = ((), (), s32[]{:S(2)}) async-start(), calls=%async_computation.1 | async-start | bytes 4325376 | tf_op jit(solution)/shard_map/reduce_scatter | solution.py:208
  23.7 14.1 %collective-permute-start = (f32[1,6,512]{2,1,0:T(8,128)S(1)}, f32[1,6,512]{2,1,0:T(8,128)S(1)}, u32[]{:S(2)}, u32[]{:S(2)}) collective-permute-start(f32[1,6,512]{2,1,0:T(8,128)S(1)} %bitcast.1602), channel_id=1, source_target_pairs={{0,32},{32,64},{64,96},{96,128},{128,160},{160,192},{192,224},{224... | collective-permute-start | bytes 36872 | tf_op jit(solution)/shard_map/ppermute | solution.py:110
  23.7 17.4 %collective-permute-start.4 = (f32[1,6,512]{2,1,0:T(8,128)S(1)}, f32[1,6,512]{2,1,0:T(8,128)S(1)}, u32[]{:S(2)}, u32[]{:S(2)}) collective-permute-start(f32[1,6,512]{2,1,0:T(8,128)S(1)} %bitcast.1603), channel_id=1, source_target_pairs={{32,0},{64,32},{96,64},{128,96},{160,128},{192,160},{224,192},{0,2... | collective-permute-start | bytes 36872 | tf_op jit(solution)/shard_map/ppermute | solution.py:114
  25.4 15.5 %collective-permute-start.7 = (f32[1,2,256]{2,0,1:T(1,128)S(1)}, f32[1,2,256]{2,0,1:T(1,128)S(1)}, u32[]{:S(2)}, u32[]{:S(2)}) collective-permute-start(f32[1,2,256]{2,0,1:T(1,128)S(1)} %copy.165), channel_id=1, source_target_pairs={{0,32},{32,64},{64,96},{96,128},{128,160},{160,192},{192,224},{1,3... | collective-permute-start | bytes 6152 | tf_op jit(solution)/shard_map/ppermute | solution.py:25
  27.4 13.6 %collective-permute-start.9 = (f32[1,2,256]{2,0,1:T(1,128)S(1)}, f32[1,2,256]{2,0,1:T(1,128)S(1)}, u32[]{:S(2)}, u32[]{:S(2)}) collective-permute-start(f32[1,2,256]{2,0,1:T(1,128)S(1)} %copy.169), channel_id=1, source_target_pairs={{32,0},{64,32},{96,64},{128,96},{160,128},{192,160},{224,192},{33,... | collective-permute-start | bytes 6152 | tf_op jit(solution)/shard_map/ppermute | solution.py:26
  37.8 3.2 collective-permute-start.1
  40.9 3.2 collective-permute-start.2
  41.1 11.5 %collective-permute-start.5 = (f32[1,6,512]{2,1,0:T(8,128)S(1)}, f32[1,6,512]{2,1,0:T(8,128)S(1)}, u32[]{:S(2)}, u32[]{:S(2)}) collective-permute-start(f32[1,6,512]{2,1,0:T(8,128)S(1)} %collective-permute-done.4), channel_id=1, source_target_pairs={{32,0},{64,32},{96,64},{128,96},{160,128},{192,160},{224,192},{0,2... | collective-permute-start | bytes 36872 | tf_op jit(solution)/shard_map/ppermute | solution.py:114
  44.1 9.9 %collective-permute-start.3 = (f32[1,6,512]{2,1,0:T(8,128)S(1)}, f32[1,6,512]{2,1,0:T(8,128)S(1)}, u32[]{:S(2)}, u32[]{:S(2)}) collective-permute-start(f32[1,6,512]{2,1,0:T(8,128)S(1)} %collective-permute-done.2), channel_id=1, source_target_pairs={{0,32},{32,64},{64,96},{96,128},{128,160},{160,192},{192,224},{224... | collective-permute-start | bytes 36872 | tf_op jit(solution)/shard_map/ppermute | solution.py:110
  45.5 33.6 %collective-permute-start.11 = (f32[514,1,256]{2,1,0:T(1,128)}, f32[514,1,256]{2,1,0:T(1,128)}, u32[]{:S(2)}, u32[]{:S(2)}) collective-permute-start(f32[514,1,256]{2,1,0:T(1,128)} %copy.175), channel_id=1, source_target_pairs={{0,1},{1,2},{2,3},{3,4},{4,5},{5,6},{6,7},{7,8},{8,9},{9,10},{10,1... | collective-permute-start | bytes 1579016 | tf_op jit(solution)/shard_map/ppermute | solution.py:25
  51.1 29.2 %collective-permute-start.13 = (f32[514,1,256]{2,1,0:T(1,128)}, f32[514,1,256]{2,1,0:T(1,128)}, u32[]{:S(2)}, u32[]{:S(2)}) collective-permute-start(f32[514,1,256]{2,1,0:T(1,128)} %copy.180), channel_id=1, source_target_pairs={{1,0},{2,1},{3,2},{4,3},{5,4},{6,5},{7,6},{8,7},{9,8},{10,9},{11,1... | collective-permute-start | bytes 1579016 | tf_op jit(solution)/shard_map/ppermute | solution.py:26
  52.5 2.9 collective-permute-start.6
  63.3 5.9 collective-permute-start.10
  66.9 4.9 collective-permute-start.8
  72.6 15.5 %collective-permute-start.12 = (f32[514,1,256]{2,1,0:T(1,128)S(1)}, f32[514,1,256]{2,1,0:T(1,128)S(1)}, u32[]{:S(2)}, u32[]{:S(2)}) collective-permute-start(f32[514,1,256]{2,1,0:T(1,128)S(1)} %copy.178), channel_id=1, source_target_pairs={{0,1},{1,2},{2,3},{3,4},{4,5},{5,6},{6,7},{7,8},{8,9},{9,10},{10,1... | collective-permute-start | bytes 1579016 | tf_op jit(solution)/shard_map/ppermute | solution.py:25
  77.8 14.9 %collective-permute-start.14 = (f32[514,1,256]{2,1,0:T(1,128)S(1)}, f32[514,1,256]{2,1,0:T(1,128)S(1)}, u32[]{:S(2)}, u32[]{:S(2)}) collective-permute-start(f32[514,1,256]{2,1,0:T(1,128)S(1)} %copy.183), channel_id=1, source_target_pairs={{1,0},{2,1},{3,2},{4,3},{5,4},{6,5},{7,6},{8,7},{9,8},{10,9},{11,1... | collective-permute-start | bytes 1579016 | tf_op jit(solution)/shard_map/ppermute | solution.py:26
  109.9 3.2 collective-permute-start.15
  113.1 3.2 collective-permute-start.16
  113.1 3.2 collective-permute-start.19
  116.3 3.2 collective-permute-start.17
  116.3 3.5 collective-permute-start.20
  119.4 3.2 collective-permute-start.18
  119.8 3.2 collective-permute-start.21
  133.1 5.6 collective-permute-start.22
  136.1 3.9 collective-permute-start.23
  140.7 14.8 %collective-permute-start.24 = (f32[514,1,256]{2,1,0:T(1,128)S(1)}, f32[514,1,256]{2,1,0:T(1,128)S(1)}, u32[]{:S(2)}, u32[]{:S(2)}) collective-permute-start(f32[514,1,256]{2,1,0:T(1,128)S(1)} %copy.198), channel_id=1, source_target_pairs={{0,1},{1,2},{2,3},{3,4},{4,5},{5,6},{6,7},{7,8},{8,9},{9,10},{10,1... | collective-permute-start | bytes 1579016 | tf_op jit(solution)/shard_map/ppermute | solution.py:25
  143.9 18.0 %collective-permute-start.25 = (f32[514,1,256]{2,1,0:T(1,128)S(1)}, f32[514,1,256]{2,1,0:T(1,128)S(1)}, u32[]{:S(2)}, u32[]{:S(2)}) collective-permute-start(f32[514,1,256]{2,1,0:T(1,128)S(1)} %copy.200), channel_id=1, source_target_pairs={{1,0},{2,1},{3,2},{4,3},{5,4},{6,5},{7,6},{8,7},{9,8},{10,9},{11,1... | collective-permute-start | bytes 1579016 | tf_op jit(solution)/shard_map/ppermute | solution.py:26
  181.2 3.2 collective-permute-start.26
  184.4 3.2 collective-permute-start.27
  184.4 3.2 collective-permute-start.30
  187.6 3.2 collective-permute-start.28
  187.6 3.2 collective-permute-start.31
  190.7 3.2 collective-permute-start.29
  190.8 3.2 collective-permute-start.32
  203.3 6.9 %collective-permute-start.33 = (f32[1,2,256]{2,0,1:T(1,128)S(1)}, f32[1,2,256]{2,0,1:T(1,128)S(1)}, u32[]{:S(2)}, u32[]{:S(2)}) collective-permute-start(f32[1,2,256]{2,0,1:T(1,128)S(1)} %get-tuple-element.212), channel_id=1, source_target_pairs={{0,32},{32,64},{64,96},{96,128},{128,160},{160,192},{192,224},{1,3... | collective-permute-start | bytes 6152 | tf_op jit(solution)/shard_map/ppermute | solution.py:25
  206.1 5.2 collective-permute-start.34
  212.0 17.4 %collective-permute-start.35 = (f32[514,1,256]{2,1,0:T(1,128)S(1)}, f32[514,1,256]{2,1,0:T(1,128)S(1)}, u32[]{:S(2)}, u32[]{:S(2)}) collective-permute-start(f32[514,1,256]{2,1,0:T(1,128)S(1)} %copy.210), channel_id=1, source_target_pairs={{0,1},{1,2},{2,3},{3,4},{4,5},{5,6},{6,7},{7,8},{8,9},{9,10},{10,1... | collective-permute-start | bytes 1579016 | tf_op jit(solution)/shard_map/ppermute | solution.py:25
  219.5 16.3 %collective-permute-start.36 = (f32[514,1,256]{2,1,0:T(1,128)}, f32[514,1,256]{2,1,0:T(1,128)}, u32[]{:S(2)}, u32[]{:S(2)}) collective-permute-start(f32[514,1,256]{2,1,0:T(1,128)} %copy.212), channel_id=1, source_target_pairs={{1,0},{2,1},{3,2},{4,3},{5,4},{6,5},{7,6},{8,7},{9,8},{10,9},{11,1... | collective-permute-start | bytes 1579016 | tf_op jit(solution)/shard_map/ppermute | solution.py:26
  246.4 337.2 %all-gather.3.cloned.1.call-start = ((), (), s32[]{:S(2)}) async-start(), calls=%async_computation.2 | async-start | bytes 4325376 | tf_op jit(solution)/shard_map/all_gather | solution.py:213
  481.1 3.0 collective-permute-start.37
  484.2 3.0 collective-permute-start.38
  484.2 3.1 collective-permute-start.41
  487.2 3.1 collective-permute-start.39
  487.2 5.1 collective-permute-start.42
  490.4 3.7 collective-permute-start.40
  492.3 5.8 collective-permute-start.43
  506.5 79.2 %copy-start.22 = (pred[256]{0:T(512)(128)(4,1)S(1)}, pred[256]{0:T(512)(128)(4,1)}, u32[]{:S(2)}) copy-start(pred[256]{0:T(512)(128)(4,1)} %compare_and_fusion) | copy-start | bytes 772
  (25 other events, 183.6 us)
Sparse Core Ops, SparseCore 0:
  246.6 232.2 reduce-scatter.1
  501.2 82.4 all-gather.2
